TPU v7x, 512 devices: a whole 4x8x8 slice. The times are simulated.
512 devices in a mesh: head: 16 (over y, core), seq: 32 (over z, x).
Axes of the slice: x: 4, y: 8, z: 8, core: 2. Of those that a mesh axis runs over, the one named last changes fastest.
Arguments:
- queries: bfloat16 [32768, 2048], P(('seq', 'head'))
- keys: bfloat16 [32768, 2048], P(('seq', 'head'))
- values: bfloat16 [32768, 2048], P(('seq', 'head')), may hold values from -6 to 6
- grad_out: bfloat16 [32768, 2048], P(('seq', 'head')), may hold values from -6 to 6
- random_blocks: int32 [256, 3], P('seq'), may hold values from 0 to 255, as said below
Outputs:
- attended: bfloat16 [32768, 2048], P(('seq', 'head'))
- grad_queries: bfloat16 [32768, 2048], P(('seq', 'head'))
- grad_keys: bfloat16 [32768, 2048], P(('seq', 'head'))
- grad_values: bfloat16 [32768, 2048], P(('seq', 'head'))
Inputs may be any that keep to these rules, and one draw needn't show every extreme that they name: `random_blocks`: within the rows of one sequence group (8 consecutive query blocks), at most 2 entries name blocks of any one group's range of 8 blocks, and in every group's rows one group's range is named exactly 2 times.
All inputs are finite; a program needn't handle non-finite values.
Results may differ from a plain program's by a relative error of at most 0.022.
Values may be sent and summed in bfloat16 or wider, within the bound.
No kernel may reach another device: no remote copies, remote signals or barrier semaphores. Data moves between devices by JAX's collectives and lax.ppermute only.
A program may use at most 192 MiB of HBM per device.

v0:
```python
import jax
import jax.numpy as jnp
from jax import lax
from jax.sharding import PartitionSpec as P

HD = 128
BLK = 128
RAND = 3


def with_halo(cells, sides, width):
    for axis, dim in sides:
        count = lax.axis_size(axis)
        ends = count - 1
        head = lax.slice_in_dim(cells, 0, width, axis=dim)
        tail = lax.slice_in_dim(cells, cells.shape[dim] - width, cells.shape[dim], axis=dim)
        cells = jnp.concatenate(
            [
                lax.ppermute(tail, axis, [(i, (i + 1) % count) for i in range(ends)]),
                cells,
                lax.ppermute(head, axis, [((i + 1) % count, i) for i in range(ends)]),
            ],
            axis=dim,
        )
    return cells


def row_width(count):
    return 4 if count % 4 == 0 else 1


def broadcast(value, axis):
    count = lax.axis_size(axis)
    me = lax.axis_index(axis)
    width = row_width(count)
    rows = count // width
    my_row = me // width
    step = 1
    while step < rows:
        pairs = [(row * width, (row + step) * width) for row in range(step) if row + step < rows]
        got = lax.ppermute(value, axis, pairs)
        arrived = (me % width == 0) & (my_row >= step) & (my_row < 2 * step)
        value = jnp.where(arrived, got, value)
        step *= 2
    got = jnp.zeros_like(value)
    for col in range(1, width):
        pairs = [(row * width, row * width + col) for row in range(rows)]
        got = got + lax.ppermute(value, axis, pairs)
    return jnp.where(me % width == 0, value, got)


def reduce_along_rows(value, axis):
    count = lax.axis_size(axis)
    width = row_width(count)
    total = value.astype(jnp.float32)
    for col in range(1, width):
        pairs = [(row * width + col, row * width) for row in range(count // width)]
        total = total + lax.ppermute(value, axis, pairs)
    return total


def reduce_row_heads(total, axis):
    count = lax.axis_size(axis)
    width = row_width(count)
    rows = count // width
    step = 1
    while step < rows:
        pairs = [((row + step) * width, row * width) for row in range(0, rows, 2 * step) if row + step < rows]
        total = total + lax.ppermute(total.astype(jnp.bfloat16), axis, pairs)
        step *= 2
    return total


def slot_places(owners, groups, capacity):
    owner_hits = (owners[:, None] == jnp.arange(groups, dtype=jnp.int32)[None, :]).astype(jnp.int32)
    earlier = jnp.cumsum(owner_hits, axis=0) - owner_hits
    return owners * capacity + jnp.sum(earlier * owner_hits, axis=1)


def request_table(list_rows, query_count, groups, capacity):
    flat_rows = list_rows.reshape(-1)
    places = slot_places(flat_rows // query_count, groups, capacity)
    matches = places[None, :] == jnp.arange(groups * capacity, dtype=jnp.int32)[:, None]
    table = jnp.sum(jnp.where(matches, (flat_rows % query_count)[None, :], 0), axis=1)
    return table.reshape(groups, capacity)


def mirror_shift(groups):
    return groups - 1


def route(list_rows, query_count, groups, capacity):
    flat_rows = list_rows.reshape(-1)
    owners = flat_rows // query_count
    places = slot_places(owners, groups, capacity)
    rank = places - owners * capacity
    source = jnp.where(rank == 0, owners, (owners + mirror_shift(groups)) % groups)
    held_id = jnp.where(rank == 0, flat_rows % query_count, query_count + flat_rows % query_count)
    hits = (source[None, :] == jnp.arange(groups, dtype=jnp.int32)[:, None]).astype(jnp.int32)
    fits = jnp.logical_and(jnp.all(jnp.sum(hits, axis=1) <= 1), jnp.all(rank <= 1))
    fast_table = jnp.sum(hits * held_id[None, :], axis=1)
    table = jnp.concatenate(
        [
            request_table(list_rows, query_count, groups, capacity),
            fast_table[:, None],
            jnp.broadcast_to(fits.astype(jnp.int32), (groups, 1)),
        ],
        axis=1,
    )
    return table, places, source


def window_valid(my_group, query_count, groups):
    block_ids = jnp.arange(query_count, dtype=jnp.int32)
    left_ok = jnp.logical_not(jnp.logical_and(my_group == 0, block_ids == 0))
    right_ok = jnp.logical_not(
        jnp.logical_and(my_group == groups - 1, block_ids == query_count - 1)
    )
    all_true = jnp.ones((query_count, BLK), dtype=bool)
    return jnp.concatenate(
        [
            all_true,
            all_true,
            left_ok[:, None] & all_true,
            all_true,
            right_ok[:, None] & all_true,
            jnp.ones((query_count, RAND * BLK), dtype=bool),
        ],
        axis=1,
    )


def against_keys(rows, global_part, window_part, remote_part):
    return jnp.concatenate(
        [
            jnp.einsum("hqid,hjd->hqij", rows, global_part, preferred_element_type=jnp.float32),
            jnp.einsum("hqid,hqjd->hqij", rows, window_part, preferred_element_type=jnp.float32),
            jnp.einsum("hqid,hqjd->hqij", rows, remote_part, preferred_element_type=jnp.float32),
        ],
        axis=-1,
    )


def split_keys(table):
    return (table[..., : 2 * BLK], table[..., 2 * BLK : 5 * BLK], table[..., 5 * BLK :])


def weigh_keys(table, global_part, window_part, remote_part):
    global_w, window_w, random_w = split_keys(table)
    return (
        jnp.einsum("hqij,hjd->hqid", global_w, global_part, preferred_element_type=jnp.float32)
        + jnp.einsum("hqij,hqjd->hqid", window_w, window_part, preferred_element_type=jnp.float32)
        + jnp.einsum("hqij,hqjd->hqid", random_w, remote_part, preferred_element_type=jnp.float32)
    )


def key_terms(table, rows):
    global_w, window_w, random_w = split_keys(table)
    return (
        jnp.einsum("hqij,hqid->hjd", global_w, rows, preferred_element_type=jnp.float32),
        jnp.einsum("hqij,hqid->hqjd", window_w, rows, preferred_element_type=jnp.float32),
        jnp.einsum("hqij,hqid->hqjd", random_w, rows, preferred_element_type=jnp.float32),
    )


def by_head(table, head_count):
    tokens = table.shape[0]
    return jnp.transpose(table.reshape(tokens, head_count, HD), (1, 0, 2))


def by_token(table):
    head_count, tokens = table.shape[0], table.shape[1]
    return jnp.transpose(table, (1, 0, 2)).reshape(tokens, head_count * HD)


def shards(queries, keys, values, grad_out, random_blocks):
    groups = lax.axis_size("seq")
    my_group = lax.axis_index("seq")
    head_q, head_k, head_v, head_g = lax.all_to_all(
        jnp.stack([queries, keys, values, grad_out]), "head", split_axis=2, concat_axis=1, tiled=True
    )
    group_tokens = head_q.shape[0]
    head_count = head_q.shape[1] // HD
    query_count = group_tokens // BLK
    capacity = max(2, 3 * query_count * RAND // (2 * groups))
    score_scale = HD ** (-0.5)
    ordered_table, places, source = route(random_blocks, query_count, groups, capacity)
    ordered_table, head_k = lax.optimization_barrier((ordered_table, head_k))
    shift = mirror_shift(groups)
    key_value = jnp.stack([by_head(head_k, head_count), by_head(head_v, head_count)])
    kv_blocks = key_value.reshape(2, head_count, query_count, BLK, HD)
    mirror = lax.ppermute(kv_blocks, "seq", [(i, (i + shift) % groups) for i in range(groups)])
    left = lax.ppermute(
        key_value[:, :, group_tokens - BLK :], "seq", [(i, i + 1) for i in range(groups - 1)]
    )
    edged = jnp.concatenate([left, key_value, mirror[:, :, 0]], axis=2)
    edged = edged.reshape(2, head_count, query_count + 2, BLK, HD)
    window_kv = jnp.concatenate(
        [edged[:, :, 0:query_count], edged[:, :, 1 : query_count + 1], edged[:, :, 2 : query_count + 2]],
        axis=3,
    )
    global_kv = broadcast(kv_blocks[:, :, 0:2].reshape(2, head_count, 2 * BLK, HD), "seq")
    received = lax.all_to_all(ordered_table, "seq", split_axis=0, concat_axis=0, tiled=True)
    wanted = received[:, :capacity]
    wanted_fast = received[:, capacity]
    take_fast = jnp.all(received[:, capacity + 1] == 1)
    held = jnp.transpose(jnp.concatenate([kv_blocks, mirror], axis=2), (2, 0, 1, 3, 4))
    held = lax.optimization_barrier(held)

    def fetch_fast(held):
        served = jnp.take(held, wanted_fast, axis=0, mode="clip")
        fetched = lax.all_to_all(served, "seq", split_axis=0, concat_axis=0, tiled=True)
        return jnp.take(fetched, source, axis=0, mode="clip")

    def fetch_all(held):
        served = jnp.take(held[:query_count], wanted.reshape(-1), axis=0, mode="clip")
        served = served.reshape(groups, capacity, 2, head_count, BLK, HD)
        fetched = lax.all_to_all(served, "seq", split_axis=0, concat_axis=0, tiled=True)
        return jnp.take(fetched.reshape(groups * capacity, 2, head_count, BLK, HD), places, axis=0, mode="clip")

    chosen = lax.cond(take_fast, fetch_fast, fetch_all, held)
    remote_kv = jnp.transpose(
        chosen.reshape(query_count, RAND, 2, head_count, BLK, HD), (2, 3, 0, 1, 4, 5)
    ).reshape(2, head_count, query_count, RAND * BLK, HD)
    query_blocks = by_head(head_q, head_count).reshape(head_count, query_count, BLK, HD)
    grad_blocks = by_head(head_g, head_count).reshape(head_count, query_count, BLK, HD)
    scores = score_scale * against_keys(query_blocks, global_kv[0], window_kv[0], remote_kv[0])
    valid = window_valid(my_group, query_count, groups)
    scores = jnp.where(valid[None, :, None, :], scores, -jnp.inf)
    row_max = jnp.max(scores, axis=-1, keepdims=True)
    exponent = jnp.exp(scores - row_max)
    attention_probs = exponent / jnp.sum(exponent, axis=-1, keepdims=True)
    weights = attention_probs.astype(jnp.bfloat16)
    attended = weigh_keys(weights, global_kv[1], window_kv[1], remote_kv[1]).astype(jnp.bfloat16)
    grad_prob = against_keys(grad_blocks, global_kv[1], window_kv[1], remote_kv[1])
    row_delta = jnp.sum(attention_probs * grad_prob, axis=-1, keepdims=True)
    grad_score = (score_scale * attention_probs * (grad_prob - row_delta)).astype(jnp.bfloat16)
    grad_q = weigh_keys(grad_score, global_kv[0], window_kv[0], remote_kv[0]).astype(jnp.bfloat16)
    key_global, key_window, key_random = key_terms(grad_score, query_blocks)
    value_global, value_window, value_random = key_terms(weights, grad_blocks)
    row_sum = reduce_along_rows(jnp.stack([key_global, value_global]).astype(jnp.bfloat16), "seq")
    window_grad = jnp.stack([key_window, value_window]).reshape(
        2, head_count, query_count, 3, BLK, HD
    )
    no_pad = (0, 0)
    extended = (
        jnp.pad(window_grad[:, :, :, 0], (no_pad, no_pad, (0, 2), no_pad, no_pad))
        + jnp.pad(window_grad[:, :, :, 1], (no_pad, no_pad, (1, 1), no_pad, no_pad))
        + jnp.pad(window_grad[:, :, :, 2], (no_pad, no_pad, (2, 0), no_pad, no_pad))
    )
    outward = jnp.concatenate([extended[:, :, 0], extended[:, :, query_count + 1]], axis=2)
    inward = with_halo(outward.astype(jnp.bfloat16), (("seq", 2),), BLK).astype(outward.dtype)
    own_grad = extended[:, :, 1 : query_count + 1]
    own_grad = own_grad.at[:, :, 0].add(inward[:, :, :BLK])
    own_grad = own_grad.at[:, :, query_count - 1].add(inward[:, :, 3 * BLK :])
    random_terms = jnp.transpose(
        jnp.stack([key_random, value_random]).reshape(2, head_count, query_count * RAND, BLK, HD),
        (2, 0, 1, 3, 4),
    ).astype(jnp.bfloat16)

    def return_fast(random_terms, row_sum):
        global_sum = reduce_row_heads(row_sum, "seq")
        send_pick = (source[None, :] == jnp.arange(groups, dtype=jnp.int32)[:, None]).astype(
            jnp.bfloat16
        )
        outgoing = jnp.einsum(
            "pj,jxhid->pxhid", send_pick, random_terms, preferred_element_type=jnp.float32
        ).astype(jnp.bfloat16)
        incoming = lax.all_to_all(outgoing, "seq", split_axis=0, concat_axis=0, tiled=True)
        take_pick = (
            wanted_fast[None, :] == jnp.arange(2 * query_count, dtype=jnp.int32)[:, None]
        ).astype(jnp.bfloat16)
        sums = jnp.einsum("qp,pxhid->xhqid", take_pick, incoming, preferred_element_type=jnp.float32)
        back = lax.ppermute(
            sums[:, :, query_count:].astype(jnp.bfloat16),
            "seq",
            [((i + shift) % groups, i) for i in range(groups)],
        )
        return sums[:, :, :query_count] + back, global_sum

    def return_all(random_terms, row_sum):
        global_sum = reduce_row_heads(row_sum, "seq")
        send_pick = (
            places[None, :] == jnp.arange(groups * capacity, dtype=jnp.int32)[:, None]
        ).astype(jnp.bfloat16)
        outgoing = jnp.einsum(
            "pj,jxhid->pxhid", send_pick, random_terms, preferred_element_type=jnp.float32
        ).astype(jnp.bfloat16)
        incoming = lax.all_to_all(
            outgoing.reshape(groups, capacity, 2, head_count, BLK, HD),
            "seq",
            split_axis=0,
            concat_axis=0,
            tiled=True,
        )
        take_pick = (
            wanted.reshape(-1)[None, :] == jnp.arange(query_count, dtype=jnp.int32)[:, None]
        ).astype(jnp.bfloat16)
        return jnp.einsum(
            "qp,pxhid->xhqid",
            take_pick,
            incoming.reshape(groups * capacity, 2, head_count, BLK, HD),
            preferred_element_type=jnp.float32,
        ), global_sum

    random_sum, global_sum = lax.cond(take_fast, return_fast, return_all, random_terms, row_sum)
    global_sum = global_sum.reshape(2, head_count, 2, BLK, HD)
    own_grad = own_grad.at[:, :, 0:2].add(jnp.where(my_group == 0, global_sum, 0.0))
    total_grad = (own_grad + random_sum).astype(jnp.bfloat16)
    flat = (head_count, group_tokens, HD)
    results = lax.all_to_all(
        jnp.stack([by_token(attended.reshape(flat)), by_token(grad_q.reshape(flat)),
                   by_token(total_grad[0].reshape(flat)), by_token(total_grad[1].reshape(flat))]),
        "head",
        split_axis=1,
        concat_axis=2,
        tiled=True,
    )
    return results[0], results[1], results[2], results[3]


def solution(mesh):
    placed = (
        P(("seq", "head"), None),
        P(("seq", "head"), None),
        P(("seq", "head"), None),
        P(("seq", "head"), None),
        P("seq", None),
    )
    return jax.shard_map(
        shards,
        mesh=mesh,
        in_specs=placed,
        out_specs=(
            P(("seq", "head"), None),
            P(("seq", "head"), None),
            P(("seq", "head"), None),
            P(("seq", "head"), None),
        ),
        check_vma=False,
    )
```

profile of v0, /device:TPU:1, one launch (start us, length us, event | category | flops | bytes accessed | tf_op | source)
XLA Modules:
  0.0 308.3 jit_solution(2477395832036208654)
XLA Ops:
  0.6 1.3 pad_maximum_fusion.3
  2.0 1.4 copy.130
  3.4 2.3 reshape.975
  5.6 10.3 %all-to-all-start.4 = ((bf16[16,2,16384]{2,1,0:T(2,128)(2,1)}), bf16[16,2,16384]{2,1,0:T(2,128)(2,1)S(1)}, u32[]{:S(2)}, u32[]{:S(2)}) async-start(bf16[16,2,16384]{2,1,0:T(2,128)(2,1)} %reshape.975), calls=%async_computation.4 | async-start | bytes 2097152 | tf_op jit(solution)/shard_map/all_to_all | solution.py:179
  16.5 0.6 compare_reduce_fusion.1
  19.7 24.2 %all-to-all-done.4 = bf16[16,2,16384]{2,1,0:T(2,128)(2,1)S(1)} async-done(((bf16[16,2,16384]{2,1,0:T(2,128)(2,1)}), bf16[16,2,16384]{2,1,0:T(2,128)(2,1)S(1)}, u32[]{:S(2)}, u32[]{:S(2)}) %all-to-all-start.4) | async-done | bytes 1048608 | tf_op jit(solution)/shard_map/all_to_all | solution.py:179
  43.9 1.3 reshape.976
  45.3 1.4 copy.131
  46.8 2.3 collective-permute-start.7
  49.1 2.5 collective-permute-done.7
  51.6 1.3 collective-permute-start.8
  53.0 0.7 copy.136
  53.7 6.4 %all-to-all-start.5 = ((s32[32,1,4]{2,1,0:T(1,128)}), s32[32,1,4]{2,1,0:T(1,128)S(1)}, u32[]{:S(2)}, u32[]{:S(2)}) async-start(s32[32,1,4]{2,1,0:T(1,128)} %copy.136), calls=%async_computation.5 | async-start | bytes 32768 | tf_op jit(solution)/shard_map/all_to_all | solution.py:203
  60.2 6.6 %collective-permute-start.14 = (bf16[2,1,8,128,128]{4,3,1,0,2:T(8,128)(2,1)S(1)}, bf16[2,1,8,128,128]{4,3,1,0,2:T(8,128)(2,1)S(1)}, u32[]{:S(2)}, u32[]{:S(2)}) collective-permute-start(bf16[2,1,8,128,128]{4,3,1,0,2:T(8,128)(2,1)S(1)} %pad_maximum_fusion.6), channel_id=1, source_target_pairs={{0,31},{1,0},{2,1},{3,2},{4,3},{5,4},{6,5},{7,6},{8,7},{9,8},{10,9... | collective-permute-start | bytes 1572872 | tf_op jit(solution)/shard_map/ppermute | solution.py:192
  66.8 4.8 %collective-permute-start.9 = (bf16[2,1,256,128]{3,2,1,0:T(8,128)(2,1)S(1)}, bf16[2,1,256,128]{3,2,1,0:T(8,128)(2,1)S(1)}, u32[]{:S(2)}, u32[]{:S(2)}) collective-permute-start(bf16[2,1,256,128]{3,2,1,0:T(8,128)(2,1)S(1)} %broadcast_select_fusion.1), channel_id=1, source_target_pairs={{0,16},{4,20},{8,24},{12,28},{32,48},{36,52},{40,56},{44,60},{64,8... | collective-permute-start | bytes 393224 | tf_op jit(solution)/shard_map/ppermute | solution.py:41
  72.2 1.9 collective-permute-start.13
  75.5 5.5 %collective-permute-start.12 = (bf16[2,1,256,128]{3,2,1,0:T(8,128)(2,1)S(1)}, bf16[2,1,256,128]{3,2,1,0:T(8,128)(2,1)S(1)}, u32[]{:S(2)}, u32[]{:S(2)}) collective-permute-start(bf16[2,1,256,128]{3,2,1,0:T(8,128)(2,1)S(1)} %broadcast_select_fusion.2), channel_id=1, source_target_pairs={{0,3},{4,7},{8,11},{12,15},{16,19},{20,23},{24,27},{28,31},{32,35}... | collective-permute-start | bytes 393224 | tf_op jit(solution)/shard_map/ppermute | solution.py:48
  81.0 1.3 collective-permute-start.11
  82.3 1.9 collective-permute-start.10
  84.4 0.7 copy-done.4
  85.2 62.3 %conditional.2 = (bf16[24,2,1,128,128]{4,3,1,0,2:T(8,128)(2,1)}) conditional(s32[]{:T(128)} %convert_element_type.174, (bf16[16,2,1,128,128]{4,3,2,1,0:T(8,128)(2,1)S(1)}, s32[32,2]{0,1:T(2,128)S(1)}, s32[24]{0:T(128)S(1)}) %tuple.79, (bf16[16,2,1,128,128]{4,3,2,1,0:T(8,128)(2,1)S(1)}, s32[32,1]{0,1:T(1,128)S(1)}, s32[24]{0:T(128)S(1)}) %tuple.39), branch_computations={%region_8.9_spmd, %region_9.10_spmd} | conditional | flops 2048 | bytes 25175784 | solution.py:221
  85.2 2.2 gather_fusion.2
  87.3 9.7 %all-to-all-start.2 = ((bf16[32,2,1,128,128]{4,3,1,2,0:T(8,128)(2,1)}), bf16[32,2,1,128,128]{4,3,1,2,0:T(8,128)(2,1)S(1)}, u32[]{:S(2)}, u32[]{:S(2)}) async-start(bf16[32,2,1,128,128]{4,3,1,2,0:T(8,128)(2,1)} %bitcast.274), calls=%async_computation.2 | async-start | bytes 4194304 | tf_op jit(solution)/shard_map/cond/branch_1_fun/all_to_all | solution.py:212
  97.6 47.8 %all-to-all-done.2 = bf16[32,2,1,128,128]{4,3,1,2,0:T(8,128)(2,1)S(1)} async-done(((bf16[32,2,1,128,128]{4,3,1,2,0:T(8,128)(2,1)}), bf16[32,2,1,128,128]{4,3,1,2,0:T(8,128)(2,1)S(1)}, u32[]{:S(2)}, u32[]{:S(2)}) %all-to-all-start.2) | async-done | bytes 2097184 | tf_op jit(solution)/shard_map/cond/branch_1_fun/all_to_all | solution.py:212
  145.3 2.1 gather_fusion.3
  147.4 1.5 copy.194
  149.1 0.9 slice_bitcast_fusion.27
  150.0 0.9 pad_maximum_fusion.5
  153.3 0.9 add_select_fusion
  155.3 1.2 fusion.26
  156.6 1.7 multiply_reduce_fusion
  158.2 1.8 multiply_convert_fusion
  160.7 1.3 collective-permute-start.18
  162.0 1.3 collective-permute-start.17
  163.3 1.3 collective-permute-start.19
  168.2 1.1 fusion.27
  169.6 1.1 fusion.28
  171.7 1.3 collective-permute-start.16
  173.0 4.0 %collective-permute-start.15 = (bf16[2,1,128,128]{3,2,0,1:T(8,128)(2,1)S(1)}, bf16[2,1,128,128]{3,2,0,1:T(8,128)(2,1)S(1)}, u32[]{:S(2)}, u32[]{:S(2)}) collective-permute-start(bf16[2,1,128,128]{3,2,0,1:T(8,128)(2,1)S(1)} %bitcast.303), channel_id=1, source_target_pairs={{0,1},{1,2},{2,3},{3,4},{4,5},{5,6},{6,7},{7,8},{8,9},{9,10},{10,1... | collective-permute-start | bytes 196616 | tf_op jit(solution)/shard_map/ppermute | solution.py:19
  177.2 1.1 collective-permute-done.15
  179.0 81.7 %conditional.3 = (f32[2,1,2,128,128]{4,3,2,0,1:T(8,128)S(1)}, f32[2,1,8,128,128]{4,3,2,1,0:T(8,128)S(1)}) conditional(s32[]{:T(128)} %convert_element_type.174, (s32[24]{0:T(128)S(1)}, bf16[24,2,1,128,128]{4,0,3,1,2:T(8,128)(2,1)S(1)}, s32[32,2]{0,1:T(2,128)S(1)}, f32[2,1,256,128]{3,2,1,0:T(8,128)S(1)}) %tuple.80, (s32[24]{0:T(128)S(1)}, ...), branch_computations={%region_13.14_spmd, %region_14.15_spmd} | conditional | flops 137299968 | bytes 46532104 | solution.py:306
  179.0 0.8 convert_bitcast_fusion
  179.8 2.2 copy.128
  182.0 12.9 %all-to-all-start = ((bf16[32,2,1,128,128]{4,3,1,2,0:T(8,128)(2,1)}), bf16[32,2,1,128,128]{4,3,1,2,0:T(8,128)(2,1)S(1)}, u32[]{:S(2)}, u32[]{:S(2)}) async-start(bf16[32,2,1,128,128]{4,3,1,2,0:T(8,128)(2,1)} %copy.128), calls=%async_computation | async-start | bytes 4194304 | tf_op jit(solution)/shard_map/cond/branch_1_fun/all_to_all | solution.py:269
  194.9 1.3 collective-permute-start.1
  196.2 45.1 %collective-permute-done.1 = bf16[2,1,256,128]{3,2,1,0:T(8,128)(2,1)S(1)} collective-permute-done((bf16[2,1,256,128]{3,2,1,0:T(8,128)(2,1)S(1)}, bf16[2,1,256,128]{3,2,1,0:T(8,128)(2,1)S(1)}, u32[]{:S(2)}, u32[]{:S(2)}) %collective-permute-start.1) | collective-permute-done | bytes 131104 | tf_op jit(solution)/shard_map/cond/branch_1_fun/ppermute | solution.py:69
  241.3 0.7 fusion.16
  242.0 1.3 collective-permute-start.2
  243.3 1.3 fusion.12
  244.6 2.8 collective-permute-start
  247.4 1.5 collective-permute-done.2
  248.9 1.0 fusion.17
  249.9 1.3 collective-permute-start.3
  251.2 8.3 %collective-permute-done.3 = bf16[2,1,256,128]{3,2,1,0:T(8,128)(2,1)S(1)} collective-permute-done((bf16[2,1,256,128]{3,2,1,0:T(8,128)(2,1)S(1)}, bf16[2,1,256,128]{3,2,1,0:T(8,128)(2,1)S(1)}, u32[]{:S(2)}, u32[]{:S(2)}) %collective-permute-start.3) | collective-permute-done | bytes 131104 | tf_op jit(solution)/shard_map/cond/branch_1_fun/ppermute | solution.py:69
  259.5 1.0 convert_add_fusion.3
  260.9 0.9 copy-done.1
  261.8 1.3 add_convert_fusion
  263.3 0.8 copy.155
  264.1 37.6 %all_to_all.58 = bf16[4,1024,128]{2,0,1:T(4,128)(2,1)S(1)} all-to-all(bf16[4,1024,128]{2,0,1:T(4,128)(2,1)S(1)} %copy.155), channel_id=1, replica_groups=mesh['head'=16,'seq'=32] {'head'}, dimensions={1} | all-to-all | bytes 2097152 | tf_op jit(solution)/shard_map/all_to_all | solution.py:311
  301.7 2.2 fusion.50
  304.3 0.8 copy.196
  305.3 0.8 copy.197
  306.4 0.8 copy.198
  307.5 0.8 copy.199
  (117 shorter events, 16.0 us)
Async XLA Ops:
  3.4 12.6 %copy-start.10 = (s32[8,3]{0,1:T(4,128)S(1)}, s32[8,3]{0,1:T(4,128)}, u32[]{:S(2)}) copy-start(s32[8,3]{0,1:T(4,128)} %param.19) | copy-start | bytes 292
  5.6 38.3 %all-to-all-start.4 = ((bf16[16,2,16384]{2,1,0:T(2,128)(2,1)}), bf16[16,2,16384]{2,1,0:T(2,128)(2,1)S(1)}, u32[]{:S(2)}, u32[]{:S(2)}) async-start(bf16[16,2,16384]{2,1,0:T(2,128)(2,1)} %reshape.975), calls=%async_computation.4 | async-start | bytes 2097152 | tf_op jit(solution)/shard_map/all_to_all | solution.py:179
  17.1 2.5 copy-start.5
  46.8 4.8 %collective-permute-start.7 = (bf16[2,1,256,128]{3,2,1,0:T(8,128)(2,1)S(1)}, bf16[2,1,256,128]{3,2,1,0:T(8,128)(2,1)S(1)}, u32[]{:S(2)}, u32[]{:S(2)}) collective-permute-start(bf16[2,1,256,128]{3,2,1,0:T(8,128)(2,1)S(1)} %bitcast.297), channel_id=1, source_target_pairs={{0,4},{32,36},{64,68},{96,100},{128,132},{160,164},{192,196},{224,... | collective-permute-start | bytes 393224 | tf_op jit(solution)/shard_map/ppermute | solution.py:41
  51.6 15.1 %collective-permute-start.8 = (bf16[2,1,256,128]{3,2,1,0:T(8,128)(2,1)S(1)}, bf16[2,1,256,128]{3,2,1,0:T(8,128)(2,1)S(1)}, u32[]{:S(2)}, u32[]{:S(2)}) collective-permute-start(bf16[2,1,256,128]{3,2,1,0:T(8,128)(2,1)S(1)} %broadcast_select_fusion), channel_id=1, source_target_pairs={{0,8},{4,12},{32,40},{36,44},{64,72},{68,76},{96,104},{100,108},{1... | collective-permute-start | bytes 393224 | tf_op jit(solution)/shard_map/ppermute | solution.py:41
  53.7 20.5 %all-to-all-start.5 = ((s32[32,1,4]{2,1,0:T(1,128)}), s32[32,1,4]{2,1,0:T(1,128)S(1)}, u32[]{:S(2)}, u32[]{:S(2)}) async-start(s32[32,1,4]{2,1,0:T(1,128)} %copy.136), calls=%async_computation.5 | async-start | bytes 32768 | tf_op jit(solution)/shard_map/all_to_all | solution.py:203
  60.1 24.3 %copy-start.6 = (s32[24]{0:T(128)S(1)}, s32[24]{0:T(128)}, u32[]{:S(2)}) copy-start(s32[24]{0:T(128)} %copy-done.5) | copy-start | bytes 292
  60.2 24.1 %collective-permute-start.14 = (bf16[2,1,8,128,128]{4,3,1,0,2:T(8,128)(2,1)S(1)}, bf16[2,1,8,128,128]{4,3,1,0,2:T(8,128)(2,1)S(1)}, u32[]{:S(2)}, u32[]{:S(2)}) collective-permute-start(bf16[2,1,8,128,128]{4,3,1,0,2:T(8,128)(2,1)S(1)} %pad_maximum_fusion.6), channel_id=1, source_target_pairs={{0,31},{1,0},{2,1},{3,2},{4,3},{5,4},{6,5},{7,6},{8,7},{9,8},{10,9... | collective-permute-start | bytes 1572872 | tf_op jit(solution)/shard_map/ppermute | solution.py:192
  66.8 8.7 %collective-permute-start.9 = (bf16[2,1,256,128]{3,2,1,0:T(8,128)(2,1)S(1)}, bf16[2,1,256,128]{3,2,1,0:T(8,128)(2,1)S(1)}, u32[]{:S(2)}, u32[]{:S(2)}) collective-permute-start(bf16[2,1,256,128]{3,2,1,0:T(8,128)(2,1)S(1)} %broadcast_select_fusion.1), channel_id=1, source_target_pairs={{0,16},{4,20},{8,24},{12,28},{32,48},{36,52},{40,56},{44,60},{64,8... | collective-permute-start | bytes 393224 | tf_op jit(solution)/shard_map/ppermute | solution.py:41
  72.2 77.8 %collective-permute-start.13 = (bf16[2,1,128,128]{3,2,0,1:T(8,128)(2,1)}, bf16[2,1,128,128]{3,2,0,1:T(8,128)(2,1)}, u32[]{:S(2)}, u32[]{:S(2)}) collective-permute-start(bf16[2,1,128,128]{3,2,0,1:T(8,128)(2,1)} %pad_maximum_fusion.10), channel_id=1, source_target_pairs={{0,1},{1,2},{2,3},{3,4},{4,5},{5,6},{6,7},{7,8},{8,9},{9,10},{10,1... | collective-permute-start | bytes 196616 | tf_op jit(solution)/shard_map/ppermute | solution.py:193
  74.2 11.0 %copy-start.8 = (s32[32,1]{0,1:T(1,128)}, s32[32,1]{0,1:T(1,128)S(1)}, u32[]{:S(2)}) copy-start(s32[32,1]{0,1:T(1,128)S(1)} %slice.248) | copy-start | bytes 388
  75.5 77.7 %collective-permute-start.12 = (bf16[2,1,256,128]{3,2,1,0:T(8,128)(2,1)S(1)}, bf16[2,1,256,128]{3,2,1,0:T(8,128)(2,1)S(1)}, u32[]{:S(2)}, u32[]{:S(2)}) collective-permute-start(bf16[2,1,256,128]{3,2,1,0:T(8,128)(2,1)S(1)} %broadcast_select_fusion.2), channel_id=1, source_target_pairs={{0,3},{4,7},{8,11},{12,15},{16,19},{20,23},{24,27},{28,31},{32,35}... | collective-permute-start | bytes 393224 | tf_op jit(solution)/shard_map/ppermute | solution.py:48
  81.0 72.2 %collective-permute-start.11 = (bf16[2,1,256,128]{3,2,1,0:T(8,128)(2,1)S(1)}, bf16[2,1,256,128]{3,2,1,0:T(8,128)(2,1)S(1)}, u32[]{:S(2)}, u32[]{:S(2)}) collective-permute-start(bf16[2,1,256,128]{3,2,1,0:T(8,128)(2,1)S(1)} %broadcast_select_fusion.2), channel_id=1, source_target_pairs={{0,2},{4,6},{8,10},{12,14},{16,18},{20,22},{24,26},{28,30},{32,34}... | collective-permute-start | bytes 393224 | tf_op jit(solution)/shard_map/ppermute | solution.py:48
  82.3 70.9 %collective-permute-start.10 = (bf16[2,1,256,128]{3,2,1,0:T(8,128)(2,1)S(1)}, bf16[2,1,256,128]{3,2,1,0:T(8,128)(2,1)}, u32[]{:S(2)}, u32[]{:S(2)}) collective-permute-start(bf16[2,1,256,128]{3,2,1,0:T(8,128)(2,1)S(1)} %broadcast_select_fusion.2), channel_id=1, source_target_pairs={{0,1},{4,5},{8,9},{12,13},{16,17},{20,21},{24,25},{28,29},{32,33},... | collective-permute-start | bytes 393224 | tf_op jit(solution)/shard_map/ppermute | solution.py:48
  84.3 0.9 copy-start.4
  87.3 58.0 %all-to-all-start.2 = ((bf16[32,2,1,128,128]{4,3,1,2,0:T(8,128)(2,1)}), bf16[32,2,1,128,128]{4,3,1,2,0:T(8,128)(2,1)S(1)}, u32[]{:S(2)}, u32[]{:S(2)}) async-start(bf16[32,2,1,128,128]{4,3,1,2,0:T(8,128)(2,1)} %bitcast.274), calls=%async_computation.2 | async-start | bytes 4194304 | tf_op jit(solution)/shard_map/cond/branch_1_fun/all_to_all | solution.py:212
  160.7 17.8 %collective-permute-start.18 = (bf16[2,1,256,128]{3,2,1,0:T(8,128)(2,1)S(1)}, bf16[2,1,256,128]{3,2,1,0:T(8,128)(2,1)S(1)}, u32[]{:S(2)}, u32[]{:S(2)}) collective-permute-start(bf16[2,1,256,128]{3,2,1,0:T(8,128)(2,1)S(1)} %pad_maximum_fusion.7), channel_id=1, source_target_pairs={{2,0},{6,4},{10,8},{14,12},{18,16},{22,20},{26,24},{30,28},{34,32}... | collective-permute-start | bytes 393224 | tf_op jit(solution)/shard_map/ppermute | solution.py:58
  162.0 16.5 %collective-permute-start.17 = (bf16[2,1,256,128]{3,2,1,0:T(8,128)(2,1)S(1)}, bf16[2,1,256,128]{3,2,1,0:T(8,128)(2,1)S(1)}, u32[]{:S(2)}, u32[]{:S(2)}) collective-permute-start(bf16[2,1,256,128]{3,2,1,0:T(8,128)(2,1)S(1)} %pad_maximum_fusion.7), channel_id=1, source_target_pairs={{1,0},{5,4},{9,8},{13,12},{17,16},{21,20},{25,24},{29,28},{33,32},... | collective-permute-start | bytes 393224 | tf_op jit(solution)/shard_map/ppermute | solution.py:58
  163.3 15.2 %collective-permute-start.19 = (bf16[2,1,256,128]{3,2,1,0:T(8,128)(2,1)S(1)}, bf16[2,1,256,128]{3,2,1,0:T(8,128)(2,1)S(1)}, u32[]{:S(2)}, u32[]{:S(2)}) collective-permute-start(bf16[2,1,256,128]{3,2,1,0:T(8,128)(2,1)S(1)} %pad_maximum_fusion.7), channel_id=1, source_target_pairs={{3,0},{7,4},{11,8},{15,12},{19,16},{23,20},{27,24},{31,28},{35,32}... | collective-permute-start | bytes 393224 | tf_op jit(solution)/shard_map/ppermute | solution.py:58
  167.9 9.1 %copy-start = (f32[2,1,10,128,128]{4,3,0,2,1:T(8,128)}, f32[2,1,10,128,128]{4,3,0,2,1:T(8,128)S(1)}, u32[]{:S(2)}) copy-start(f32[2,1,10,128,128]{4,3,0,2,1:T(8,128)S(1)} %pad_add_fusion) | copy-start | bytes 3932164
  171.7 5.5 %collective-permute-start.16 = (bf16[2,1,128,128]{3,2,0,1:T(8,128)(2,1)S(1)}, bf16[2,1,128,128]{3,2,0,1:T(8,128)(2,1)S(1)}, u32[]{:S(2)}, u32[]{:S(2)}) collective-permute-start(bf16[2,1,128,128]{3,2,0,1:T(8,128)(2,1)S(1)} %bitcast.305), channel_id=1, source_target_pairs={{1,0},{2,1},{3,2},{4,3},{5,4},{6,5},{7,6},{8,7},{9,8},{10,9},{11,1... | collective-permute-start | bytes 196616 | tf_op jit(solution)/shard_map/ppermute | solution.py:21
  173.0 5.3 %collective-permute-start.15 = (bf16[2,1,128,128]{3,2,0,1:T(8,128)(2,1)S(1)}, bf16[2,1,128,128]{3,2,0,1:T(8,128)(2,1)S(1)}, u32[]{:S(2)}, u32[]{:S(2)}) collective-permute-start(bf16[2,1,128,128]{3,2,0,1:T(8,128)(2,1)S(1)} %bitcast.303), channel_id=1, source_target_pairs={{0,1},{1,2},{2,3},{3,4},{4,5},{5,6},{6,7},{7,8},{8,9},{9,10},{10,1... | collective-permute-start | bytes 196616 | tf_op jit(solution)/shard_map/ppermute | solution.py:19
  177.0 1.3 slice-start
  178.4 0.7 copy-start.7
  178.4 0.6 copy-start.9
  182.0 61.3 %all-to-all-start = ((bf16[32,2,1,128,128]{4,3,1,2,0:T(8,128)(2,1)}), bf16[32,2,1,128,128]{4,3,1,2,0:T(8,128)(2,1)S(1)}, u32[]{:S(2)}, u32[]{:S(2)}) async-start(bf16[32,2,1,128,128]{4,3,1,2,0:T(8,128)(2,1)} %copy.128), calls=%async_computation | async-start | bytes 4194304 | tf_op jit(solution)/shard_map/cond/branch_1_fun/all_to_all | solution.py:269
  194.9 46.4 %collective-permute-start.1 = (bf16[2,1,256,128]{3,2,1,0:T(8,128)(2,1)S(1)}, bf16[2,1,256,128]{3,2,1,0:T(8,128)(2,1)S(1)}, u32[]{:S(2)}, u32[]{:S(2)}) collective-permute-start(bf16[2,1,256,128]{3,2,1,0:T(8,128)(2,1)S(1)} %convert_element_type.150), channel_id=1, source_target_pairs={{4,0},{12,8},{20,16},{28,24},{36,32},{44,40},{52,48},{60,56},{68,6... | collective-permute-start | bytes 393224 | tf_op jit(solution)/shard_map/cond/branch_1_fun/ppermute | solution.py:69
  242.0 6.9 %collective-permute-start.2 = (bf16[2,1,256,128]{3,2,1,0:T(8,128)(2,1)}, bf16[2,1,256,128]{3,2,1,0:T(8,128)(2,1)}, u32[]{:S(2)}, u32[]{:S(2)}) collective-permute-start(bf16[2,1,256,128]{3,2,1,0:T(8,128)(2,1)} %fusion.16), channel_id=1, source_target_pairs={{8,0},{24,16},{40,32},{56,48},{72,64},{88,80},{104,96},{120,112},{... | collective-permute-start | bytes 393224 | tf_op jit(solution)/shard_map/cond/branch_1_fun/ppermute | solution.py:69
  244.6 15.8 %collective-permute-start = (bf16[2,1,8,128,128]{4,2,3,0,1:T(8,128)(2,1)S(1)}, bf16[2,1,8,128,128]{4,2,3,0,1:T(8,128)(2,1)S(1)}, u32[]{:S(2)}, u32[]{:S(2)}) collective-permute-start(bf16[2,1,8,128,128]{4,2,3,0,1:T(8,128)(2,1)S(1)} %slice.378), channel_id=1, source_target_pairs={{31,0},{0,1},{1,2},{2,3},{3,4},{4,5},{5,6},{6,7},{7,8},{8,9},{9,10... | collective-permute-start | bytes 1572872 | tf_op jit(solution)/shard_map/cond/branch_1_fun/ppermute | solution.py:274
  249.9 9.6 %collective-permute-start.3 = (bf16[2,1,256,128]{3,2,1,0:T(8,128)(2,1)S(1)}, bf16[2,1,256,128]{3,2,1,0:T(8,128)(2,1)S(1)}, u32[]{:S(2)}, u32[]{:S(2)}) collective-permute-start(bf16[2,1,256,128]{3,2,1,0:T(8,128)(2,1)S(1)} %fusion.17), channel_id=1, source_target_pairs={{16,0},{48,32},{80,64},{112,96},{144,128},{176,160},{208,192},{240... | collective-permute-start | bytes 393224 | tf_op jit(solution)/shard_map/cond/branch_1_fun/ppermute | solution.py:69
  260.8 1.0 copy-start.1
  260.8 2.4 copy-start.2
  260.8 2.4 copy-start.3
where the time goes:
time: 309 us; the launch traced here: 308 us
  waiting for transfers between devices  131 us (42%)
  starting transfers between devices  80.6 us (26%)
  blocking collectives  37.6 us (12%)
  local copies, waits for them, and re-layouts  28.2 us (9%)
  other arithmetic  17.5 us (6%)
  matrix products  10.4 us (3%)
  between operations  3.3 us (1%)
    ppermute x3, waiting for transfers between devices, reduce_row_heads(): total = total + lax.ppermute(total.astype(jnp.bfloat16), axis, pairs)  54.9 us
    all_to_all x1, waiting for transfers between devices, fetch_fast(): lax.all_to_all(served, 'seq', split_axis=0, concat_axis=0, tiled=True)  47.8 us
    all_to_all x1, blocking collectives, shards(): lax.all_to_all(jnp.stack([by_token(attended.reshape(flat)), by_token(grad...  37.6 us
    all_to_all x1, waiting for transfers between devices, shards(): lax.all_to_all(jnp.stack([queries, keys, values, grad_out]), 'head', spli...  24.2 us
    all_to_all x1, starting transfers between devices, return_fast(): lax.all_to_all(outgoing, 'seq', split_axis=0, concat_axis=0, tiled=True)  12.9 us
    all_to_all x1, starting transfers between devices, shards(): lax.all_to_all(jnp.stack([queries, keys, values, grad_out]), 'head', spli...  10.3 us
    all_to_all x1, starting transfers between devices, fetch_fast(): lax.all_to_all(served, 'seq', split_axis=0, concat_axis=0, tiled=True)  9.65 us
    unnamed x34, local copies, waits for them, and re-layouts  9.1 us
  transfers between devices with their start and end apart: 21, of which 7 were waited for; matrix products, arithmetic and copies ran while one was open for 9% of the time, Pallas kernels for 0%

commit v1 on v0

--- a/solution.py
+++ b/solution.py
@@ -251,8 +251,9 @@
     outward = jnp.concatenate([extended[:, :, 0], extended[:, :, query_count + 1]], axis=2)
     inward = with_halo(outward.astype(jnp.bfloat16), (("seq", 2),), BLK).astype(outward.dtype)
     own_grad = extended[:, :, 1 : query_count + 1]
-    own_grad = own_grad.at[:, :, 0].add(inward[:, :, :BLK])
-    own_grad = own_grad.at[:, :, query_count - 1].add(inward[:, :, 3 * BLK :])
+    edge_pad = ((0, 0), (0, 0), (0, query_count - 1), (0, 0), (0, 0))
+    own_grad = own_grad + jnp.pad(inward[:, :, None, :BLK], edge_pad)
+    own_grad = own_grad + jnp.pad(inward[:, :, None, 3 * BLK :], (edge_pad[0], edge_pad[1], (query_count - 1, 0), edge_pad[3], edge_pad[4]))
     random_terms = jnp.transpose(
         jnp.stack([key_random, value_random]).reshape(2, head_count, query_count * RAND, BLK, HD),
         (2, 0, 1, 3, 4),
@@ -305,7 +306,9 @@
 
     random_sum, global_sum = lax.cond(take_fast, return_fast, return_all, random_terms, row_sum)
     global_sum = global_sum.reshape(2, head_count, 2, BLK, HD)
-    own_grad = own_grad.at[:, :, 0:2].add(jnp.where(my_group == 0, global_sum, 0.0))
+    own_grad = own_grad + jnp.pad(
+        jnp.where(my_group == 0, global_sum, 0.0), ((0, 0), (0, 0), (0, query_count - 2), (0, 0), (0, 0))
+    )
     total_grad = (own_grad + random_sum).astype(jnp.bfloat16)
     flat = (head_count, group_tokens, HD)
     results = lax.all_to_all(

time: 309 us -> 307 us (level)
    unnamed x34 -> x30, local copies, waits for them, and re-layouts: 9.1 us -> 7.78 us
  transfers between devices with their start and end apart: 21 -> 21, of which waited for: 7 -> 7; matrix products, arithmetic and copies ran while one was open for 9% -> 8% of each run, Pallas kernels for 0% -> 0%
where the time goes in v1:
time: 307 us; the launch traced here: 306 us
  waiting for transfers between devices  130 us (42%)
  starting transfers between devices  81.3 us (26%)
  blocking collectives  36.9 us (12%)
  local copies, waits for them, and re-layouts  26.8 us (9%)
  other arithmetic  16.9 us (6%)
  matrix products  10.4 us (3%)
  between operations  3.25 us (1%)
    ppermute x3, waiting for transfers between devices, reduce_row_heads(): total = total + lax.ppermute(total.astype(jnp.bfloat16), axis, pairs)  54.6 us
    all_to_all x1, waiting for transfers between devices, fetch_fast(): lax.all_to_all(served, 'seq', split_axis=0, concat_axis=0, tiled=True)  47.8 us
    all_to_all x1, blocking collectives, shards(): lax.all_to_all(jnp.stack([by_token(attended.reshape(flat)), by_token(grad...  36.9 us
    all_to_all x1, waiting for transfers between devices, shards(): lax.all_to_all(jnp.stack([queries, keys, values, grad_out]), 'head', spli...  24.2 us
    all_to_all x1, starting transfers between devices, return_fast(): lax.all_to_all(outgoing, 'seq', split_axis=0, concat_axis=0, tiled=True)  12.9 us
    all_to_all x1, starting transfers between devices, shards(): lax.all_to_all(jnp.stack([queries, keys, values, grad_out]), 'head', spli...  10.3 us
    all_to_all x1, starting transfers between devices, fetch_fast(): lax.all_to_all(served, 'seq', split_axis=0, concat_axis=0, tiled=True)  9.65 us
    ppermute x3, starting transfers between devices, broadcast(): got = got + lax.ppermute(value, axis, pairs)  8.76 us
  transfers between devices with their start and end apart: 21, of which 7 were waited for; matrix products, arithmetic and copies ran while one was open for 8% of the time, Pallas kernels for 0%

profile of v1, /device:TPU:1, one launch (start us, length us, event | category | flops | bytes accessed | tf_op | source)
XLA Modules:
  0.0 306.1 jit_solution(16641712376933975458)
XLA Ops:
  0.6 1.3 pad_maximum_fusion.3
  2.0 1.4 copy.126
  3.4 2.3 reshape.852
  5.6 10.3 %all-to-all-start.4 = ((bf16[16,2,16384]{2,1,0:T(2,128)(2,1)}), bf16[16,2,16384]{2,1,0:T(2,128)(2,1)S(1)}, u32[]{:S(2)}, u32[]{:S(2)}) async-start(bf16[16,2,16384]{2,1,0:T(2,128)(2,1)} %reshape.852), calls=%async_computation.4 | async-start | bytes 2097152 | tf_op jit(solution)/shard_map/all_to_all | solution.py:179
  16.5 0.6 compare_reduce_fusion.1
  17.2 0.6 compare_reduce_fusion.2
  19.7 24.2 %all-to-all-done.4 = bf16[16,2,16384]{2,1,0:T(2,128)(2,1)S(1)} async-done(((bf16[16,2,16384]{2,1,0:T(2,128)(2,1)}), bf16[16,2,16384]{2,1,0:T(2,128)(2,1)S(1)}, u32[]{:S(2)}, u32[]{:S(2)}) %all-to-all-start.4) | async-done | bytes 1048608 | tf_op jit(solution)/shard_map/all_to_all | solution.py:179
  43.9 1.3 reshape.853
  45.3 1.4 copy.127
  46.7 2.3 collective-permute-start.7
  49.1 2.5 collective-permute-done.7
  51.6 1.3 collective-permute-start.8
  52.9 0.7 copy.132
  53.6 6.4 %all-to-all-start.5 = ((s32[32,1,4]{2,1,0:T(1,128)}), s32[32,1,4]{2,1,0:T(1,128)S(1)}, u32[]{:S(2)}, u32[]{:S(2)}) async-start(s32[32,1,4]{2,1,0:T(1,128)} %copy.132), calls=%async_computation.5 | async-start | bytes 32768 | tf_op jit(solution)/shard_map/all_to_all | solution.py:203
  60.1 6.6 %collective-permute-start.14 = (bf16[2,1,8,128,128]{4,3,1,0,2:T(8,128)(2,1)S(1)}, bf16[2,1,8,128,128]{4,3,1,0,2:T(8,128)(2,1)S(1)}, u32[]{:S(2)}, u32[]{:S(2)}) collective-permute-start(bf16[2,1,8,128,128]{4,3,1,0,2:T(8,128)(2,1)S(1)} %pad_maximum_fusion.6), channel_id=1, source_target_pairs={{0,31},{1,0},{2,1},{3,2},{4,3},{5,4},{6,5},{7,6},{8,7},{9,8},{10,9... | collective-permute-start | bytes 1572872 | tf_op jit(solution)/shard_map/ppermute | solution.py:192
  66.7 4.8 %collective-permute-start.9 = (bf16[2,1,256,128]{3,2,1,0:T(8,128)(2,1)S(1)}, bf16[2,1,256,128]{3,2,1,0:T(8,128)(2,1)S(1)}, u32[]{:S(2)}, u32[]{:S(2)}) collective-permute-start(bf16[2,1,256,128]{3,2,1,0:T(8,128)(2,1)S(1)} %broadcast_select_fusion.1), channel_id=1, source_target_pairs={{0,16},{4,20},{8,24},{12,28},{32,48},{36,52},{40,56},{44,60},{64,8... | collective-permute-start | bytes 393224 | tf_op jit(solution)/shard_map/ppermute | solution.py:41
  72.2 1.9 collective-permute-start.13
  74.2 0.6 compare_reduce_fusion
  75.5 5.5 %collective-permute-start.12 = (bf16[2,1,256,128]{3,2,1,0:T(8,128)(2,1)S(1)}, bf16[2,1,256,128]{3,2,1,0:T(8,128)(2,1)S(1)}, u32[]{:S(2)}, u32[]{:S(2)}) collective-permute-start(bf16[2,1,256,128]{3,2,1,0:T(8,128)(2,1)S(1)} %broadcast_select_fusion.2), channel_id=1, source_target_pairs={{0,3},{4,7},{8,11},{12,15},{16,19},{20,23},{24,27},{28,31},{32,35}... | collective-permute-start | bytes 393224 | tf_op jit(solution)/shard_map/ppermute | solution.py:48
  81.0 1.3 collective-permute-start.11
  82.3 2.0 collective-permute-start.10
  84.4 0.7 copy-done.2
  85.2 62.3 %conditional.2 = (bf16[24,2,1,128,128]{4,3,1,0,2:T(8,128)(2,1)}) conditional(s32[]{:T(128)} %convert_element_type.180, (bf16[16,2,1,128,128]{4,3,2,1,0:T(8,128)(2,1)S(1)}, s32[32,2]{0,1:T(2,128)S(1)}, s32[24]{0:T(128)S(1)}) %tuple.68, (bf16[16,2,1,128,128]{4,3,2,1,0:T(8,128)(2,1)S(1)}, s32[32,1]{0,1:T(1,128)S(1)}, s32[24]{0:T(128)S(1)}) %tuple.27), branch_computations={%region_8.9_spmd, %region_9.10_spmd} | conditional | flops 2048 | bytes 25175784 | solution.py:221
  85.2 2.1 gather_fusion.2
  87.3 9.7 %all-to-all-start.2 = ((bf16[32,2,1,128,128]{4,3,1,2,0:T(8,128)(2,1)}), bf16[32,2,1,128,128]{4,3,1,2,0:T(8,128)(2,1)S(1)}, u32[]{:S(2)}, u32[]{:S(2)}) async-start(bf16[32,2,1,128,128]{4,3,1,2,0:T(8,128)(2,1)} %bitcast.261), calls=%async_computation.2 | async-start | bytes 4194304 | tf_op jit(solution)/shard_map/cond/branch_1_fun/all_to_all | solution.py:212
  97.6 47.8 %all-to-all-done.2 = bf16[32,2,1,128,128]{4,3,1,2,0:T(8,128)(2,1)S(1)} async-done(((bf16[32,2,1,128,128]{4,3,1,2,0:T(8,128)(2,1)}), bf16[32,2,1,128,128]{4,3,1,2,0:T(8,128)(2,1)S(1)}, u32[]{:S(2)}, u32[]{:S(2)}) %all-to-all-start.2) | async-done | bytes 2097184 | tf_op jit(solution)/shard_map/cond/branch_1_fun/all_to_all | solution.py:212
  145.3 2.1 gather_fusion.3
  147.4 1.5 copy.196
  149.1 0.9 slice_bitcast_fusion.26
  150.0 0.9 pad_maximum_fusion.5
  153.3 0.9 add_select_fusion
  155.3 1.2 fusion.26
  156.6 1.7 multiply_reduce_fusion
  158.3 1.8 multiply_convert_fusion
  160.7 1.3 collective-permute-start.18
  162.0 1.3 collective-permute-start.17
  163.3 1.3 collective-permute-start.19
  167.7 1.3 pad_add_fusion
  169.3 1.1 fusion.27
  170.7 1.1 fusion.28
  172.8 1.3 collective-permute-start.16
  174.1 4.0 %collective-permute-start.15 = (bf16[2,1,128,128]{3,2,0,1:T(8,128)(2,1)S(1)}, bf16[2,1,128,128]{3,2,0,1:T(8,128)(2,1)S(1)}, u32[]{:S(2)}, u32[]{:S(2)}) collective-permute-start(bf16[2,1,128,128]{3,2,0,1:T(8,128)(2,1)S(1)} %bitcast.290), channel_id=1, source_target_pairs={{0,1},{1,2},{2,3},{3,4},{4,5},{5,6},{6,7},{7,8},{8,9},{9,10},{10,1... | collective-permute-start | bytes 196616 | tf_op jit(solution)/shard_map/ppermute | solution.py:19
  178.3 1.1 collective-permute-done.15
  179.4 0.7 convert_bitcast_fusion.2
  180.2 79.9 %conditional.3 = (f32[2,1,2,128,128]{4,3,2,0,1:T(8,128)S(1)}, f32[2,1,8,128,128]{4,3,2,1,0:T(8,128)S(1)}) conditional(s32[]{:T(128)} %convert_element_type.180, (s32[24]{0:T(128)S(1)}, bf16[24,2,1,128,128]{4,0,3,1,2:T(8,128)(2,1)S(1)}, s32[32,2]{0,1:T(2,128)S(1)}, f32[2,1,256,128]{3,2,1,0:T(8,128)S(1)}) %tuple.69, (s32[24]{0:T(128)S(1)}, ...), branch_computations={%region_13.14_spmd, %region_14.15_spmd} | conditional | flops 137299968 | bytes 46532104 | solution.py:307
  180.5 0.8 convert_bitcast_fusion
  181.3 2.1 copy.124
  183.4 12.9 %all-to-all-start = ((bf16[32,2,1,128,128]{4,3,1,2,0:T(8,128)(2,1)}), bf16[32,2,1,128,128]{4,3,1,2,0:T(8,128)(2,1)S(1)}, u32[]{:S(2)}, u32[]{:S(2)}) async-start(bf16[32,2,1,128,128]{4,3,1,2,0:T(8,128)(2,1)} %copy.124), calls=%async_computation | async-start | bytes 4194304 | tf_op jit(solution)/shard_map/cond/branch_1_fun/all_to_all | solution.py:270
  196.3 1.3 collective-permute-start.1
  197.6 45.1 %collective-permute-done.1 = bf16[2,1,256,128]{3,2,1,0:T(8,128)(2,1)S(1)} collective-permute-done((bf16[2,1,256,128]{3,2,1,0:T(8,128)(2,1)S(1)}, bf16[2,1,256,128]{3,2,1,0:T(8,128)(2,1)S(1)}, u32[]{:S(2)}, u32[]{:S(2)}) %collective-permute-start.1) | collective-permute-done | bytes 131104 | tf_op jit(solution)/shard_map/cond/branch_1_fun/ppermute | solution.py:69
  242.8 1.3 collective-permute-start.2
  244.1 1.3 fusion.12
  245.4 3.4 %collective-permute-start = (bf16[2,1,8,128,128]{4,2,3,0,1:T(8,128)(2,1)S(1)}, bf16[2,1,8,128,128]{4,2,3,0,1:T(8,128)(2,1)S(1)}, u32[]{:S(2)}, u32[]{:S(2)}) collective-permute-start(bf16[2,1,8,128,128]{4,2,3,0,1:T(8,128)(2,1)S(1)} %slice.267), channel_id=1, source_target_pairs={{31,0},{0,1},{1,2},{2,3},{3,4},{4,5},{5,6},{6,7},{7,8},{8,9},{9,10... | collective-permute-start | bytes 1572872 | tf_op jit(solution)/shard_map/cond/branch_1_fun/ppermute | solution.py:275
  248.8 1.2 collective-permute-done.2
  250.1 1.3 collective-permute-start.3
  251.4 8.3 %collective-permute-done.3 = bf16[2,1,256,128]{3,2,1,0:T(8,128)(2,1)S(1)} collective-permute-done((bf16[2,1,256,128]{3,2,1,0:T(8,128)(2,1)S(1)}, bf16[2,1,256,128]{3,2,1,0:T(8,128)(2,1)S(1)}, u32[]{:S(2)}, u32[]{:S(2)}) %collective-permute-start.3) | collective-permute-done | bytes 131104 | tf_op jit(solution)/shard_map/cond/branch_1_fun/ppermute | solution.py:69
  260.1 1.5 fusion.37
  261.8 0.8 copy.150
  262.6 36.9 %all_to_all.58 = bf16[4,1024,128]{2,0,1:T(4,128)(2,1)S(1)} all-to-all(bf16[4,1024,128]{2,0,1:T(4,128)(2,1)S(1)} %copy.150), channel_id=1, replica_groups=mesh['head'=16,'seq'=32] {'head'}, dimensions={1} | all-to-all | bytes 2097152 | tf_op jit(solution)/shard_map/all_to_all | solution.py:314
  299.6 2.2 fusion.48
  302.1 0.8 copy.198
  303.2 0.8 copy.199
  304.3 0.8 copy.200
  305.4 0.8 copy.201
  (109 shorter events, 14.1 us)
Async XLA Ops:
  3.4 12.6 %copy-start.8 = (s32[8,3]{0,1:T(4,128)S(1)}, s32[8,3]{0,1:T(4,128)}, u32[]{:S(2)}) copy-start(s32[8,3]{0,1:T(4,128)} %param.13) | copy-start | bytes 292
  5.6 38.3 %all-to-all-start.4 = ((bf16[16,2,16384]{2,1,0:T(2,128)(2,1)}), bf16[16,2,16384]{2,1,0:T(2,128)(2,1)S(1)}, u32[]{:S(2)}, u32[]{:S(2)}) async-start(bf16[16,2,16384]{2,1,0:T(2,128)(2,1)} %reshape.852), calls=%async_computation.4 | async-start | bytes 2097152 | tf_op jit(solution)/shard_map/all_to_all | solution.py:179
  17.1 2.5 copy-start.3
  46.7 4.8 %collective-permute-start.7 = (bf16[2,1,256,128]{3,2,1,0:T(8,128)(2,1)S(1)}, bf16[2,1,256,128]{3,2,1,0:T(8,128)(2,1)S(1)}, u32[]{:S(2)}, u32[]{:S(2)}) collective-permute-start(bf16[2,1,256,128]{3,2,1,0:T(8,128)(2,1)S(1)} %bitcast.284), channel_id=1, source_target_pairs={{0,4},{32,36},{64,68},{96,100},{128,132},{160,164},{192,196},{224,... | collective-permute-start | bytes 393224 | tf_op jit(solution)/shard_map/ppermute | solution.py:41
  51.6 15.1 %collective-permute-start.8 = (bf16[2,1,256,128]{3,2,1,0:T(8,128)(2,1)S(1)}, bf16[2,1,256,128]{3,2,1,0:T(8,128)(2,1)S(1)}, u32[]{:S(2)}, u32[]{:S(2)}) collective-permute-start(bf16[2,1,256,128]{3,2,1,0:T(8,128)(2,1)S(1)} %broadcast_select_fusion), channel_id=1, source_target_pairs={{0,8},{4,12},{32,40},{36,44},{64,72},{68,76},{96,104},{100,108},{1... | collective-permute-start | bytes 393224 | tf_op jit(solution)/shard_map/ppermute | solution.py:41
  53.6 20.5 %all-to-all-start.5 = ((s32[32,1,4]{2,1,0:T(1,128)}), s32[32,1,4]{2,1,0:T(1,128)S(1)}, u32[]{:S(2)}, u32[]{:S(2)}) async-start(s32[32,1,4]{2,1,0:T(1,128)} %copy.132), calls=%async_computation.5 | async-start | bytes 32768 | tf_op jit(solution)/shard_map/all_to_all | solution.py:203
  60.1 24.3 %copy-start.4 = (s32[24]{0:T(128)S(1)}, s32[24]{0:T(128)}, u32[]{:S(2)}) copy-start(s32[24]{0:T(128)} %copy-done.3) | copy-start | bytes 292
  60.1 24.1 %collective-permute-start.14 = (bf16[2,1,8,128,128]{4,3,1,0,2:T(8,128)(2,1)S(1)}, bf16[2,1,8,128,128]{4,3,1,0,2:T(8,128)(2,1)S(1)}, u32[]{:S(2)}, u32[]{:S(2)}) collective-permute-start(bf16[2,1,8,128,128]{4,3,1,0,2:T(8,128)(2,1)S(1)} %pad_maximum_fusion.6), channel_id=1, source_target_pairs={{0,31},{1,0},{2,1},{3,2},{4,3},{5,4},{6,5},{7,6},{8,7},{9,8},{10,9... | collective-permute-start | bytes 1572872 | tf_op jit(solution)/shard_map/ppermute | solution.py:192
  66.7 8.7 %collective-permute-start.9 = (bf16[2,1,256,128]{3,2,1,0:T(8,128)(2,1)S(1)}, bf16[2,1,256,128]{3,2,1,0:T(8,128)(2,1)S(1)}, u32[]{:S(2)}, u32[]{:S(2)}) collective-permute-start(bf16[2,1,256,128]{3,2,1,0:T(8,128)(2,1)S(1)} %broadcast_select_fusion.1), channel_id=1, source_target_pairs={{0,16},{4,20},{8,24},{12,28},{32,48},{36,52},{40,56},{44,60},{64,8... | collective-permute-start | bytes 393224 | tf_op jit(solution)/shard_map/ppermute | solution.py:41
  72.2 77.8 %collective-permute-start.13 = (bf16[2,1,128,128]{3,2,0,1:T(8,128)(2,1)}, bf16[2,1,128,128]{3,2,0,1:T(8,128)(2,1)}, u32[]{:S(2)}, u32[]{:S(2)}) collective-permute-start(bf16[2,1,128,128]{3,2,0,1:T(8,128)(2,1)} %pad_maximum_fusion.10), channel_id=1, source_target_pairs={{0,1},{1,2},{2,3},{3,4},{4,5},{5,6},{6,7},{7,8},{8,9},{9,10},{10,1... | collective-permute-start | bytes 196616 | tf_op jit(solution)/shard_map/ppermute | solution.py:193
  74.2 11.0 %copy-start.6 = (s32[32,1]{0,1:T(1,128)}, s32[32,1]{0,1:T(1,128)S(1)}, u32[]{:S(2)}) copy-start(s32[32,1]{0,1:T(1,128)S(1)} %slice.149) | copy-start | bytes 388
  75.5 77.7 %collective-permute-start.12 = (bf16[2,1,256,128]{3,2,1,0:T(8,128)(2,1)S(1)}, bf16[2,1,256,128]{3,2,1,0:T(8,128)(2,1)S(1)}, u32[]{:S(2)}, u32[]{:S(2)}) collective-permute-start(bf16[2,1,256,128]{3,2,1,0:T(8,128)(2,1)S(1)} %broadcast_select_fusion.2), channel_id=1, source_target_pairs={{0,3},{4,7},{8,11},{12,15},{16,19},{20,23},{24,27},{28,31},{32,35}... | collective-permute-start | bytes 393224 | tf_op jit(solution)/shard_map/ppermute | solution.py:48
  81.0 72.2 %collective-permute-start.11 = (bf16[2,1,256,128]{3,2,1,0:T(8,128)(2,1)S(1)}, bf16[2,1,256,128]{3,2,1,0:T(8,128)(2,1)S(1)}, u32[]{:S(2)}, u32[]{:S(2)}) collective-permute-start(bf16[2,1,256,128]{3,2,1,0:T(8,128)(2,1)S(1)} %broadcast_select_fusion.2), channel_id=1, source_target_pairs={{0,2},{4,6},{8,10},{12,14},{16,18},{20,22},{24,26},{28,30},{32,34}... | collective-permute-start | bytes 393224 | tf_op jit(solution)/shard_map/ppermute | solution.py:48
  82.3 70.9 %collective-permute-start.10 = (bf16[2,1,256,128]{3,2,1,0:T(8,128)(2,1)S(1)}, bf16[2,1,256,128]{3,2,1,0:T(8,128)(2,1)}, u32[]{:S(2)}, u32[]{:S(2)}) collective-permute-start(bf16[2,1,256,128]{3,2,1,0:T(8,128)(2,1)S(1)} %broadcast_select_fusion.2), channel_id=1, source_target_pairs={{0,1},{4,5},{8,9},{12,13},{16,17},{20,21},{24,25},{28,29},{32,33},... | collective-permute-start | bytes 393224 | tf_op jit(solution)/shard_map/ppermute | solution.py:48
  84.3 0.9 copy-start.2
  87.3 58.0 %all-to-all-start.2 = ((bf16[32,2,1,128,128]{4,3,1,2,0:T(8,128)(2,1)}), bf16[32,2,1,128,128]{4,3,1,2,0:T(8,128)(2,1)S(1)}, u32[]{:S(2)}, u32[]{:S(2)}) async-start(bf16[32,2,1,128,128]{4,3,1,2,0:T(8,128)(2,1)} %bitcast.261), calls=%async_computation.2 | async-start | bytes 4194304 | tf_op jit(solution)/shard_map/cond/branch_1_fun/all_to_all | solution.py:212
  160.7 19.4 %collective-permute-start.18 = (bf16[2,1,256,128]{3,2,1,0:T(8,128)(2,1)S(1)}, bf16[2,1,256,128]{3,2,1,0:T(8,128)(2,1)S(1)}, u32[]{:S(2)}, u32[]{:S(2)}) collective-permute-start(bf16[2,1,256,128]{3,2,1,0:T(8,128)(2,1)S(1)} %pad_maximum_fusion.7), channel_id=1, source_target_pairs={{2,0},{6,4},{10,8},{14,12},{18,16},{22,20},{26,24},{30,28},{34,32}... | collective-permute-start | bytes 393224 | tf_op jit(solution)/shard_map/ppermute | solution.py:58
  162.0 18.1 %collective-permute-start.17 = (bf16[2,1,256,128]{3,2,1,0:T(8,128)(2,1)S(1)}, bf16[2,1,256,128]{3,2,1,0:T(8,128)(2,1)S(1)}, u32[]{:S(2)}, u32[]{:S(2)}) collective-permute-start(bf16[2,1,256,128]{3,2,1,0:T(8,128)(2,1)S(1)} %pad_maximum_fusion.7), channel_id=1, source_target_pairs={{1,0},{5,4},{9,8},{13,12},{17,16},{21,20},{25,24},{29,28},{33,32},... | collective-permute-start | bytes 393224 | tf_op jit(solution)/shard_map/ppermute | solution.py:58
  163.3 16.8 %collective-permute-start.19 = (bf16[2,1,256,128]{3,2,1,0:T(8,128)(2,1)S(1)}, bf16[2,1,256,128]{3,2,1,0:T(8,128)(2,1)S(1)}, u32[]{:S(2)}, u32[]{:S(2)}) collective-permute-start(bf16[2,1,256,128]{3,2,1,0:T(8,128)(2,1)S(1)} %pad_maximum_fusion.7), channel_id=1, source_target_pairs={{3,0},{7,4},{11,8},{15,12},{19,16},{23,20},{27,24},{31,28},{35,32}... | collective-permute-start | bytes 393224 | tf_op jit(solution)/shard_map/ppermute | solution.py:58
  172.8 5.5 %collective-permute-start.16 = (bf16[2,1,128,128]{3,2,0,1:T(8,128)(2,1)S(1)}, bf16[2,1,128,128]{3,2,0,1:T(8,128)(2,1)S(1)}, u32[]{:S(2)}, u32[]{:S(2)}) collective-permute-start(bf16[2,1,128,128]{3,2,0,1:T(8,128)(2,1)S(1)} %bitcast.292), channel_id=1, source_target_pairs={{1,0},{2,1},{3,2},{4,3},{5,4},{6,5},{7,6},{8,7},{9,8},{10,9},{11,1... | collective-permute-start | bytes 196616 | tf_op jit(solution)/shard_map/ppermute | solution.py:21
  174.1 6.1 %copy-start.5 = (s32[24]{0:T(128)S(1)}, s32[24]{0:T(128)}, u32[]{:S(2)}) copy-start(s32[24]{0:T(128)} %copy-done.3) | copy-start | bytes 292
  174.1 6.1 %copy-start.7 = (s32[32,1]{0,1:T(1,128)S(1)}, s32[32,1]{0,1:T(1,128)}, u32[]{:S(2)}) copy-start(s32[32,1]{0,1:T(1,128)} %copy-done.6) | copy-start | bytes 388
  174.1 5.3 %collective-permute-start.15 = (bf16[2,1,128,128]{3,2,0,1:T(8,128)(2,1)S(1)}, bf16[2,1,128,128]{3,2,0,1:T(8,128)(2,1)S(1)}, u32[]{:S(2)}, u32[]{:S(2)}) collective-permute-start(bf16[2,1,128,128]{3,2,0,1:T(8,128)(2,1)S(1)} %bitcast.290), channel_id=1, source_target_pairs={{0,1},{1,2},{2,3},{3,4},{4,5},{5,6},{6,7},{7,8},{8,9},{9,10},{10,1... | collective-permute-start | bytes 196616 | tf_op jit(solution)/shard_map/ppermute | solution.py:19
  183.4 60.7 %all-to-all-start = ((bf16[32,2,1,128,128]{4,3,1,2,0:T(8,128)(2,1)}), bf16[32,2,1,128,128]{4,3,1,2,0:T(8,128)(2,1)S(1)}, u32[]{:S(2)}, u32[]{:S(2)}) async-start(bf16[32,2,1,128,128]{4,3,1,2,0:T(8,128)(2,1)} %copy.124), calls=%async_computation | async-start | bytes 4194304 | tf_op jit(solution)/shard_map/cond/branch_1_fun/all_to_all | solution.py:270
  196.3 46.4 %collective-permute-start.1 = (bf16[2,1,256,128]{3,2,1,0:T(8,128)(2,1)S(1)}, bf16[2,1,256,128]{3,2,1,0:T(8,128)(2,1)S(1)}, u32[]{:S(2)}, u32[]{:S(2)}) collective-permute-start(bf16[2,1,256,128]{3,2,1,0:T(8,128)(2,1)S(1)} %convert_element_type.156), channel_id=1, source_target_pairs={{4,0},{12,8},{20,16},{28,24},{36,32},{44,40},{52,48},{60,56},{68,6... | collective-permute-start | bytes 393224 | tf_op jit(solution)/shard_map/cond/branch_1_fun/ppermute | solution.py:69
  242.8 7.3 %collective-permute-start.2 = (bf16[2,1,256,128]{3,2,1,0:T(8,128)(2,1)S(1)}, bf16[2,1,256,128]{3,2,1,0:T(8,128)(2,1)S(1)}, u32[]{:S(2)}, u32[]{:S(2)}) collective-permute-start(bf16[2,1,256,128]{3,2,1,0:T(8,128)(2,1)S(1)} %fusion.16), channel_id=1, source_target_pairs={{8,0},{24,16},{40,32},{56,48},{72,64},{88,80},{104,96},{120,112},{... | collective-permute-start | bytes 393224 | tf_op jit(solution)/shard_map/cond/branch_1_fun/ppermute | solution.py:69
  245.4 14.4 %collective-permute-start = (bf16[2,1,8,128,128]{4,2,3,0,1:T(8,128)(2,1)S(1)}, bf16[2,1,8,128,128]{4,2,3,0,1:T(8,128)(2,1)S(1)}, u32[]{:S(2)}, u32[]{:S(2)}) collective-permute-start(bf16[2,1,8,128,128]{4,2,3,0,1:T(8,128)(2,1)S(1)} %slice.267), channel_id=1, source_target_pairs={{31,0},{0,1},{1,2},{2,3},{3,4},{4,5},{5,6},{6,7},{7,8},{8,9},{9,10... | collective-permute-start | bytes 1572872 | tf_op jit(solution)/shard_map/cond/branch_1_fun/ppermute | solution.py:275
  250.1 9.6 %collective-permute-start.3 = (bf16[2,1,256,128]{3,2,1,0:T(8,128)(2,1)S(1)}, bf16[2,1,256,128]{3,2,1,0:T(8,128)(2,1)S(1)}, u32[]{:S(2)}, u32[]{:S(2)}) collective-permute-start(bf16[2,1,256,128]{3,2,1,0:T(8,128)(2,1)S(1)} %fusion.17), channel_id=1, source_target_pairs={{16,0},{48,32},{80,64},{112,96},{144,128},{176,160},{208,192},{240... | collective-permute-start | bytes 393224 | tf_op jit(solution)/shard_map/cond/branch_1_fun/ppermute | solution.py:69
  260.1 1.5 copy-start
  260.1 1.5 copy-start.1
